TPU v7x, 32 devices: a whole 2x2x4 slice. The times are simulated.
32 devices in a mesh: layer: 4 (over x, core), tok: 8 (over z, y).
Axes of the slice: x: 2, y: 2, z: 4, core: 2. Of those that a mesh axis runs over, the one named last changes fastest.
Arguments:
- active_codes: bfloat16 [4, 1024, 32], P('layer', 'tok'), may hold values from 0.19921875 to 3
- latent_ids: int32 [4, 1024, 32], P('layer', 'tok'), may hold values from 0 to 32767, as said below
- decoder: bfloat16 [4, 32768, 4096], P('layer', 'tok'), may hold values from -1 to 1
- carry_gain: float32 [4, 4096], P('layer'), may hold values from 0.1 to 1
- earlier_sum: bfloat16 [1024, 4096], P('tok'), may hold values from -6 to 6
- targets: bfloat16 [4, 1024, 4096], P('layer', 'tok'), may hold values from -6 to 6
Outputs:
- reconstruction: bfloat16 [4, 1024, 4096], P('layer', 'tok')
- code_grad: float32 [4, 1024, 32], P('layer', 'tok')
Inputs may be any that keep to these rules, and one draw needn't show every extreme that they name: `latent_ids`: A token's 32 ids in one layer are distinct. In each layer, the 128 tokens of one aligned block have at most 768 ids in any one range of 4096 consecutive latents, and in every layer one range holds exactly 768 ids of every block.
All inputs are finite; a program needn't handle non-finite values.
Results may differ from a plain program's by a relative error of at most 0.019.
Values may be sent and summed in bfloat16 or wider, within the bound.
No kernel may reach another device: no remote copies, remote signals or barrier semaphores. Data moves between devices by JAX's collectives and lax.ppermute only.
A program may use at most 256 MiB of HBM per device.

v0:
```python
import jax
import jax.numpy as jnp
from jax import lax
from jax.sharding import PartitionSpec as P


def prefix(shard, axis, combine, identity, reverse):
    length, mine = (lax.axis_size(axis), lax.axis_index(axis))
    everything = jax.tree.map(
        lambda part, kind: lax.all_gather(part.astype(kind), axis),
        shard,
        (jnp.bfloat16, jnp.bfloat16),
    )
    start = jax.tree.map(
        lambda part, zero: jnp.broadcast_to(jnp.asarray(zero, part.dtype), part.shape),
        shard,
        identity,
    )

    def lap(k, before):
        at = length - 1 - k if reverse else k
        reached = at > mine if reverse else at < mine
        new = combine(
            before, jax.tree.map(lambda part, own: part[at].astype(own.dtype), everything, shard)
        )
        return jax.tree.map(lambda a, b: jnp.where(reached, a, b), new, before)

    return lax.fori_loop(0, length, lap, start)


def bucket_lists(latent_rows, code_rows, range_size, owners, capacity):
    tok_rows, top_count = latent_rows.shape
    entries = tok_rows * top_count
    flat_ids = latent_rows.reshape(entries)
    owning = flat_ids // range_size
    within = flat_ids % range_size
    positions = jnp.arange(entries, dtype=jnp.int32) // top_count
    ordering = jnp.argsort(owning, stable=True)
    counts = jnp.sum(
        (owning[:, None] == jnp.arange(owners, dtype=jnp.int32)[None, :]).astype(jnp.int32), axis=0
    )
    starts = jnp.cumsum(counts) - counts
    sorted_rank = jnp.arange(entries, dtype=jnp.int32) - starts[owning[ordering]]
    rank_of = jnp.zeros(entries, jnp.int32).at[ordering].set(sorted_rank)
    slot_index = owning * capacity + rank_of
    slot_keys = (
        jnp.zeros(owners * capacity, jnp.int32).at[slot_index].set(within * tok_rows + positions)
    )
    slot_codes = (
        jnp.zeros(owners * capacity, jnp.bfloat16).at[slot_index].set(code_rows.reshape(entries))
    )
    return (slot_keys.reshape(owners, capacity), slot_codes.reshape(owners, capacity), slot_index)


def source_term(rows, slot_keys, slot_codes, tok_rows):
    token_index = slot_keys % tok_rows
    matches = token_index[None, :] == jnp.arange(tok_rows, dtype=jnp.int32)[:, None]
    spread = jnp.where(matches, slot_codes[None, :], jnp.zeros((), jnp.bfloat16))
    return jnp.dot(spread, rows, preferred_element_type=jnp.float32)


def slot_grads_of(rows, slot_keys, grad_block, tok_rows):
    token_index = slot_keys % tok_rows
    products = jnp.einsum("td,cd->tc", grad_block, rows, preferred_element_type=jnp.float32)
    matches = token_index[None, :] == jnp.arange(tok_rows, dtype=jnp.int32)[:, None]
    return jnp.sum(jnp.where(matches, products, 0.0), axis=0)


def compose(earlier_part, later_part):
    return (earlier_part[0] * later_part[0], later_part[0] * earlier_part[1] + later_part[1])


def on_device(active_codes, latent_ids, decoder, carry_gain, earlier_sum, targets):
    owners = lax.axis_size("tok")
    tok_rows = active_codes.shape[1]
    top_count = active_codes.shape[2]
    range_size = decoder.shape[1]
    model_width = decoder.shape[2]
    capacity = 3 * tok_rows * top_count // (2 * owners)
    weights = decoder[0]
    slot_keys, slot_codes, slot_index = bucket_lists(
        latent_ids[0], active_codes[0], range_size, owners, capacity
    )
    recv_keys, recv_codes = (
        lax.all_to_all(slot_keys, "tok", split_axis=0, concat_axis=0, tiled=True),
        lax.all_to_all(slot_codes, "tok", split_axis=0, concat_axis=0, tiled=True),
    )
    row_cache = jnp.take(weights, recv_keys // tok_rows, axis=0)

    def one_source(triple):
        return source_term(triple[2], triple[0], triple[1], tok_rows)

    keys_part = recv_keys
    rows_part = row_cache
    term_blocks = lax.map(one_source, (keys_part, recv_codes, rows_part))
    decoded = lax.psum_scatter(
        term_blocks.reshape(lax.axis_size("tok") * tok_rows, model_width).astype(jnp.bfloat16),
        "tok",
        scatter_dimension=0,
        tiled=True,
    ).astype(jnp.float32)
    identity = (jnp.ones_like(carry_gain), jnp.zeros_like(decoded))
    ahead_gain, ahead_sum = prefix((carry_gain, decoded), "layer", compose, identity, False)
    recon_full = carry_gain * (ahead_gain * earlier_sum.astype(jnp.float32) + ahead_sum) + decoded
    misfit = recon_full - targets[0].astype(jnp.float32)
    behind_gain, behind_sum = prefix(
        (carry_gain, carry_gain * misfit), "layer", compose, identity, True
    )
    grad_low = (misfit + behind_sum).astype(jnp.bfloat16)

    def grads_of_source(triple):
        return slot_grads_of(triple[2], triple[0], triple[1], tok_rows)

    segment = lax.all_gather(grad_low, "tok", axis=0, tiled=True)
    source_count = segment.shape[0] // tok_rows
    keys_part = recv_keys
    rows_part = row_cache
    grad_blocks = segment.reshape(source_count, tok_rows, model_width)
    values = lax.map(grads_of_source, (keys_part, grad_blocks, rows_part))
    returned = lax.all_to_all(values, "tok", split_axis=0, concat_axis=0, tiled=True)
    code_grad = jnp.take(returned.reshape(owners * capacity), slot_index).reshape(
        tok_rows, top_count
    )
    return (recon_full.astype(jnp.bfloat16)[None], code_grad[None])


def solution(mesh):
    return jax.shard_map(
        on_device,
        mesh=mesh,
        in_specs=(
            P("layer", "tok", None),
            P("layer", "tok", None),
            P("layer", "tok", None),
            P("layer", None),
            P("tok", None),
            P("layer", "tok", None),
        ),
        out_specs=(P("layer", "tok", None), P("layer", "tok", None)),
        check_vma=False,
    )
```

profile of v0, /device:TPU:0, one launch (start us, length us, event | category | flops | bytes accessed | tf_op | source)
XLA Modules:
  0.0 932.6 jit_solution(17020449953633308792)
XLA Ops:
  9.1 5.8 sort.17
  14.9 23.0 %gather_fusion = s32[4096]{0:T(1024)S(1)} fusion(s32[4096]{0:T(1024)S(1)} %add_select_fusion.3, s32[4096]{0:T(1024)S(1)} %get-tuple-element.481), kind=kCustom, calls=%fused_computation | custom fusion | bytes 49152 | tf_op jit(solution)/shard_map/gather | solution.py:43
  43.0 15.5 %scatter_custom_fusion = s32[4096]{0:T(1024)S(1)} fusion(s32[4096]{0:T(1024)S(1)} %get-tuple-element.482, s32[4096]{0:T(1024)S(1)} %select_subtract_fusion, s32[]{:T(128)} %constant.237.clone.1), kind=kCustom, calls=%fused_computation.106 | custom fusion | bytes 16388 | tf_op jit(solution)/shard_map/scatter | solution.py:44
  59.4 28.6 %scatter_custom_fusion.2 = bf16[6144]{0:T(1024)(128)(2,1)S(1)} fusion(s32[4096]{0:T(1024)S(1)} %get-tuple-element.475, bf16[4096]{0:T(1024)(128)(2,1)S(1)} %reshape.307, bf16[]{:T(256)} %constant.252.clone.1), kind=kCustom, calls=%fused_computation.108 | custom fusion | bytes 12290 | tf_op jit(solution)/shard_map/scatter | solution.py:50
  89.9 7.3 all-to-all-start.1
  97.1 16.1 %scatter_custom_fusion.1 = s32[6144]{0:T(1024)} fusion(s32[4096]{0:T(1024)S(1)} %get-tuple-element.475, s32[4096]{0:T(1024)S(1)} %get-tuple-element.480, s32[]{:T(128)} %constant.237.clone.1), kind=kCustom, calls=%fused_computation.101 | custom fusion | bytes 24580 | tf_op jit(solution)/shard_map/scatter | solution.py:47
  113.2 6.0 all-to-all-start
  120.1 5.8 all-to-all-done
  126.0 262.2 %gather_fusion.1 = bf16[6144,4096]{1,0:T(8,128)(2,1)} fusion(bf16[4096,4096]{1,0:T(8,128)(2,1)} %bitcast.100, s32[6144]{0:T(1024)S(1)} %broadcast_clamp_fusion), kind=kCustom, calls=%fused_computation.1 | custom fusion | bytes 100687872 | tf_op jit(solution)/shard_map/jit(_take)/gather | solution.py:88
  388.3 33.4 %broadcast_select_fusion.2 = bf16[8,768,4096]{2,1,0:T(8,128)(2,1)} fusion(bf16[8,768,4096]{2,1,0:T(8,128)(2,1)} %bitcast.101, pred[8,768]{1,0:T(8,128)(4,1)S(1)} %compare_and_fusion), kind=kLoop, calls=%fused_computation.46 | loop fusion | flops 25165824 | bytes 100669440 | tf_op jit(solution)/shard_map/jit(_take)/select_n | solution.py:88
  421.7 44.3 %while.56 = (s32[]{:T(128)}, bf16[8,128,4096]{2,1,0:T(8,128)(2,1)}, s32[8,768]{1,0:T(8,128)S(1)}, bf16[8,768]{1,0:T(8,128)(2,1)}, bf16[8,768,4096]{2,1,0:T(8,128)(2,1)}, /*index=5*/s32[]{:T(128)}) while((s32[]{:T(128)}, bf16[8,128,4096]{2,1,0:T(8,128)(2,1)}, s32[8,768]{1,0:T(8,128)S(1)}, bf16[8,768]{1,0:T(8,128)(2,1)}, ...), condition=%wide.region_7.8_spmd, body=%wide.region_6.7_spmd.sunk | while | flops 805511424 | bytes 8403533 | solution.py:95
  433.5 4.8 fusion.63
  450.1 4.8 fusion.63
  461.2 4.8 fusion.63
  466.0 159.1 %reduce-scatter.2.cloned.1.call-done = bf16[128,4096]{1,0:T(8,128)(2,1)} async-done(((bf16[1024,4096]{1,0:T(8,128)(2,1)}), bf16[128,4096]{1,0:T(8,128)(2,1)}) %reduce-scatter.2.cloned.1.call-update) | async-done | bytes 1048592 | tf_op jit(solution)/shard_map/reduce_scatter | solution.py:96
  625.2 5.2 all-gather.3
  630.5 29.8 %all-gather.10.cloned.1.call-done = bf16[512,4096]{1,0:T(8,128)(2,1)} async-done(((bf16[128,4096]{1,0:T(8,128)(2,1)}), bf16[512,4096]{1,0:T(8,128)(2,1)}) %all-gather.10.cloned.1.call-update) | async-done | bytes 4194320 | tf_op jit(solution)/shard_map/all_gather | solution.py:10
  660.2 10.5 %while.58 = (s32[]{:T(128)}, f32[1,4096]{1,0:T(1,128)S(1)}, f32[128,4096]{1,0:T(8,128)S(1)}, s32[]{:T(128)}, bf16[4,1,4096]{2,1,0:T(2,128)(2,1)S(1)}, /*index=5*/bf16[4,128,4096]{2,1,0:T(8,128)(2,1)}, s32[]{:T(128)}, s32[]{:T(128)}) while((s32[]{:T(128)}, f32[1,4096]{1,0:T(1,128)S(1)}, f32[128,4096]{1,0:T(8,128)S(1)}, ...), condition=%wide.region_10.11_spmd.clone, body=%wide.region_9.10_spmd.clone.sunk | while | flops 2637828 | bytes 5316723 | solution.py:28
  674.8 34.6 %all-gather.12.cloned.1.call-done = bf16[512,4096]{1,0:T(8,128)(2,1)} async-done(((bf16[128,4096]{1,0:T(8,128)(2,1)}), bf16[512,4096]{1,0:T(8,128)(2,1)}) %all-gather.12.cloned.1.call-update) | async-done | bytes 4194320 | tf_op jit(solution)/shard_map/all_gather | solution.py:10
  709.3 10.4 %while.59 = (s32[]{:T(128)}, f32[128,4096]{1,0:T(8,128)S(1)}, s32[]{:T(128)}, bf16[4,1,4096]{2,1,0:T(2,128)(2,1)S(1)}, bf16[4,128,4096]{2,1,0:T(8,128)(2,1)}, /*index=5*/s32[]{:T(128)}, s32[]{:T(128)}, s32[]{:T(128)}, s32[]{:T(128)}) while((s32[]{:T(128)}, f32[128,4096]{1,0:T(8,128)S(1)}, s32[]{:T(128)}, ...), condition=%wide.region_12.13_spmd.clone, body=%wide.region_11.12_spmd.clone.sunk | while | flops 2625544 | bytes 5284007 | solution.py:28
  723.9 125.1 %all-gather.8.cloned.1.call-done = bf16[1024,4096]{1,0:T(8,128)(2,1)} async-done(((bf16[128,4096]{1,0:T(8,128)(2,1)}), bf16[1024,4096]{1,0:T(8,128)(2,1)}) %all-gather.8.cloned.1.call-update) | async-done | bytes 8388624 | tf_op jit(solution)/shard_map/all_gather | solution.py:114
  849.0 44.0 %while.57 = (s32[]{:T(128)}, f32[8,768]{1,0:T(8,128)S(1)}, s32[8,768]{1,0:T(8,128)S(1)}, bf16[8,128,4096]{2,1,0:T(8,128)(2,1)}, bf16[8,768,4096]{2,1,0:T(8,128)(2,1)}, /*index=5*/s32[]{:T(128)}, s32[]{:T(128)}) while((s32[]{:T(128)}, f32[8,768]{1,0:T(8,128)S(1)}, s32[8,768]{1,0:T(8,128)S(1)}, bf16[8,128,4096]{2,1,0:T(8,128)(2,1)}, ...), condition=%wide.region_15.16_spmd, body=%wide.region_13.15_spmd.sunk | while | flops 805608960 | bytes 7365717 | solution.py:119
  849.0 5.3 fusion.67
  854.5 5.3 fusion.67
  860.0 5.3 fusion.67
  865.5 5.3 fusion.67
  871.0 5.3 fusion.67
  876.5 5.3 fusion.67
  882.0 5.3 fusion.67
  887.6 5.3 fusion.67
  893.0 9.2 all_to_all.37
  902.3 23.0 %gather_fusion.2 = f32[4096]{0:T(1024)S(1)} fusion(f32[6144]{0:T(1024)S(1)} %bitcast.99, s32[4096]{0:T(1024)S(1)} %copy-done.4), kind=kCustom, calls=%fused_computation.2 | custom fusion | bytes 49152 | tf_op jit(solution)/shard_map/jit(_take)/gather | solution.py:121
  (119 shorter events, 71.2 us)
Async XLA Ops:
  14.9 44.3 %copy-start.5 = (bf16[1,128,32]{1,2,0:T(8,128)(2,1)S(1)}, bf16[1,128,32]{1,2,0:T(8,128)(2,1)}, u32[]{:S(2)}) copy-start(bf16[1,128,32]{1,2,0:T(8,128)(2,1)} %param.14) | copy-start | bytes 24580
  59.2 60.3 %copy-start.2 = (s32[4096]{0:T(1024)}, s32[4096]{0:T(1024)S(1)}, u32[]{:S(2)}) copy-start(s32[4096]{0:T(1024)S(1)} %get-tuple-element.475) | copy-start | bytes 49156
  89.9 23.4 %all-to-all-start.1 = ((bf16[8,2,384]{2,1,0:T(2,128)(2,1)}), bf16[8,2,384]{2,1,0:T(2,128)(2,1)S(1)}, u32[]{:S(2)}, u32[]{:S(2)}) async-start(bf16[8,2,384]{2,1,0:T(2,128)(2,1)} %reshape.367), calls=%async_computation.1 | async-start | bytes 24576 | tf_op jit(solution)/shard_map/all_to_all | solution.py:86
  113.2 12.6 %all-to-all-start = ((s32[8,1,768]{2,1,0:T(1,128)}), s32[8,1,768]{2,1,0:T(1,128)S(1)}, u32[]{:S(2)}, u32[]{:S(2)}) async-start(s32[8,1,768]{2,1,0:T(1,128)} %bitcast.18), calls=%async_computation | async-start | bytes 49152 | tf_op jit(solution)/shard_map/all_to_all | solution.py:85
  119.2 505.9 %reduce-scatter.2.cloned.1.call-start = ((), (), s32[]{:S(2)}) async-start(), calls=%async_computation.4 | async-start | bytes 9437184 | tf_op jit(solution)/shard_map/reduce_scatter | solution.py:96
  466.0 159.2 %copy-start.1 = (f32[1,4096]{1,0:T(1,128)S(1)}, f32[1,4096]{1,0:T(1,128)}, u32[]{:S(2)}) copy-start(f32[1,4096]{1,0:T(1,128)} %param.17) | copy-start | bytes 49156
  466.0 194.3 %all-gather.10.cloned.1.call-start = ((), (), s32[]{:S(2)}) async-start(), calls=%async_computation.6 | async-start | bytes 5242880 | tf_op jit(solution)/shard_map/all_gather | solution.py:10
  625.1 84.2 %all-gather.12.cloned.1.call-start = ((), (), s32[]{:S(2)}) async-start(), calls=%async_computation.7 | async-start | bytes 5242880 | tf_op jit(solution)/shard_map/all_gather | solution.py:10
  660.2 10.6 %copy-start = (bf16[1,128,4096]{2,1,0:T(8,128)(2,1)S(1)}, bf16[1,128,4096]{2,1,0:T(8,128)(2,1)}, u32[]{:S(2)}) copy-start(bf16[1,128,4096]{2,1,0:T(8,128)(2,1)} %param.19) | copy-start | bytes 3145732
  674.7 174.3 %all-gather.8.cloned.1.call-start = ((), (), s32[]{:S(2)}) async-start(), calls=%async_computation.5 | async-start | bytes 9437184 | tf_op jit(solution)/shard_map/all_gather | solution.py:114
  849.0 53.3 %copy-start.4 = (s32[4096]{0:T(1024)S(1)}, s32[4096]{0:T(1024)}, u32[]{:S(2)}) copy-start(s32[4096]{0:T(1024)} %get-tuple-element.474) | copy-start | bytes 49156
  902.3 23.0 %copy-start.3 = (s32[4096]{0:T(1024)S(1)}, s32[4096]{0:T(1024)}, u32[]{:S(2)}) copy-start(s32[4096]{0:T(1024)} %copy-done.2) | copy-start | bytes 49156
Sparse Core Ops, SparseCore 0:
  466.1 158.9 reduce-scatter.1
  626.7 33.4 all-gather.9
  674.8 34.4 all-gather.11
  724.0 124.9 all-gather.7
where the time goes:
time: 940 us; the launch traced here: 933 us
  local copies, waits for them, and re-layouts  379 us (40%)
  waiting for transfers between devices  354 us (38%)
  matrix products  80.9 us (9%)
  other arithmetic  75.3 us (8%)
  blocking collectives  14.5 us (2%)
  between operations  14 us (1%)
  starting transfers between devices  13.6 us (1%)
    gather x1, local copies, waits for them, and re-layouts, on_device(): row_cache = jnp.take(weights, recv_keys // tok_rows, axis=0)  262 us
    reduce_scatter x1, waiting for transfers between devices, on_device(): lax.psum_scatter(term_blocks.reshape(lax.axis_size('tok') * tok_rows, mod...  159 us
    all_gather x1, waiting for transfers between devices, on_device(): segment = lax.all_gather(grad_low, 'tok', axis=0, tiled=True)  125 us
    all_gather x2, waiting for transfers between devices, prefix(): lax.all_gather(part.astype(kind), axis)  64.4 us
    dot_general x8, matrix products, slot_grads_of(): jnp.einsum('td,cd->tc', grad_block, rows, preferred_element_type=jnp.floa...  42.8 us
    dot_general x8, matrix products, source_term(): return jnp.dot(spread, rows, preferred_element_type=jnp.float32)  38.1 us
    select_n x2, other arithmetic, on_device(): row_cache = jnp.take(weights, recv_keys // tok_rows, axis=0)  33.5 us
    scatter x1, local copies, waits for them, and re-layouts, bucket_lists(): jnp.zeros(owners * capacity, jnp.bfloat16).at[slot_index]  28.6 us
  transfers between devices with their start and end apart: 6, of which 5 were waited for; matrix products, arithmetic and copies ran while one was open for 2% of the time, Pallas kernels for 0%

commit v1 on v0

--- a/solution.py
+++ b/solution.py
@@ -111,7 +111,22 @@
     def grads_of_source(triple):
         return slot_grads_of(triple[2], triple[0], triple[1], tok_rows)
 
-    segment = lax.all_gather(grad_low, "tok", axis=0, tiled=True)
+    ways, here, step = (lax.axis_size("tok"), lax.axis_index("tok"), grad_low.shape[0])
+    shape = [n * ways if d == 0 else n for d, n in enumerate(grad_low.shape)]
+    segment = lax.dynamic_update_slice_in_dim(
+        jnp.zeros(shape, grad_low.dtype), grad_low, here * step, axis=0
+    )
+    going_up = going_down = grad_low
+    for far in range(1, ways // 2 + 1):
+        going_up = lax.ppermute(going_up, "tok", [(d, (d + 1) % ways) for d in range(ways)])
+        segment = lax.dynamic_update_slice_in_dim(
+            segment, going_up, (here - far) % ways * step, axis=0
+        )
+        if 2 * far < ways:
+            going_down = lax.ppermute(going_down, "tok", [(d, (d - 1) % ways) for d in range(ways)])
+            segment = lax.dynamic_update_slice_in_dim(
+                segment, going_down, (here + far) % ways * step, axis=0
+            )
     source_count = segment.shape[0] // tok_rows
     keys_part = recv_keys
     rows_part = row_cache

time: 940 us -> 985 us (1.048)
  waiting for transfers between devices: 354 us -> 376 us
  starting transfers between devices: 13.6 us -> 34.6 us
  local copies, waits for them, and re-layouts: 379 us -> 394 us
    ppermute x0 -> x7, waiting for transfers between devices: none -> 141 us  [the longest x4 141 us: on_device(): lax.ppermute(going_up, 'tok', [(d, (d + 1) % ways) for d in range(ways)])]
    all_gather x1 -> x0, waiting for transfers between devices: 125 us -> none  [on_device(): segment = lax.all_gather(grad_low, 'tok', axis=0, tiled=True)]
    ppermute x0 -> x7, starting transfers between devices: none -> 17.7 us  [the longest x4 8.92 us: on_device(): lax.ppermute(going_up, 'tok', [(d, (d + 1) % ways) for d in range(ways)])]
  transfers between devices with their start and end apart: 6 -> 13, of which waited for: 5 -> 9; matrix products, arithmetic and copies ran while one was open for 2% -> 3% of each run, Pallas kernels for 0% -> 0%
where the time goes in v1:
time: 985 us; the launch traced here: 978 us
  local copies, waits for them, and re-layouts  394 us (40%)
  waiting for transfers between devices  376 us (38%)
  matrix products  81 us (8%)
  other arithmetic  72.8 us (7%)
  starting transfers between devices  34.6 us (4%)
  between operations  14 us (1%)
    gather x1, local copies, waits for them, and re-layouts, on_device(): row_cache = jnp.take(weights, recv_keys // tok_rows, axis=0)  262 us
    reduce_scatter x1, waiting for transfers between devices, on_device(): lax.psum_scatter(term_blocks.reshape(lax.axis_size('tok') * tok_rows, mod...  159 us
    ppermute x4, waiting for transfers between devices, on_device(): lax.ppermute(going_up, 'tok', [(d, (d + 1) % ways) for d in range(ways)])  141 us
    all_gather x2, waiting for transfers between devices, prefix(): lax.all_gather(part.astype(kind), axis)  64.4 us
    dot_general x8, matrix products, slot_grads_of(): jnp.einsum('td,cd->tc', grad_block, rows, preferred_element_type=jnp.floa...  42.9 us
    dot_general x8, matrix products, source_term(): return jnp.dot(spread, rows, preferred_element_type=jnp.float32)  38.2 us
    select_n x2, other arithmetic, on_device(): row_cache = jnp.take(weights, recv_keys // tok_rows, axis=0)  33.5 us
    scatter x1, local copies, waits for them, and re-layouts, bucket_lists(): jnp.zeros(owners * capacity, jnp.bfloat16).at[slot_index]  28.6 us
  transfers between devices with their start and end apart: 13, of which 9 were waited for; matrix products, arithmetic and copies ran while one was open for 3% of the time, Pallas kernels for 0%

profile of v1, /device:TPU:0, one launch (start us, length us, event | category | flops | bytes accessed | tf_op | source)
XLA Modules:
  0.0 977.8 jit_solution(5083424700576341078)
XLA Ops:
  9.1 5.8 sort.17
  14.9 23.0 %gather_fusion = s32[4096]{0:T(1024)S(1)} fusion(s32[4096]{0:T(1024)S(1)} %add_select_fusion.3, s32[4096]{0:T(1024)S(1)} %get-tuple-element.481), kind=kCustom, calls=%fused_computation | custom fusion | bytes 49152 | tf_op jit(solution)/shard_map/gather | solution.py:43
  43.0 15.5 %scatter_custom_fusion = s32[4096]{0:T(1024)S(1)} fusion(s32[4096]{0:T(1024)S(1)} %get-tuple-element.482, s32[4096]{0:T(1024)S(1)} %select_subtract_fusion, s32[]{:T(128)} %constant.283.clone.1), kind=kCustom, calls=%fused_computation.106 | custom fusion | bytes 16388 | tf_op jit(solution)/shard_map/scatter | solution.py:44
  59.4 28.6 %scatter_custom_fusion.2 = bf16[6144]{0:T(1024)(128)(2,1)S(1)} fusion(s32[4096]{0:T(1024)S(1)} %get-tuple-element.475, bf16[4096]{0:T(1024)(128)(2,1)S(1)} %reshape.307, bf16[]{:T(256)} %constant.298.clone.1), kind=kCustom, calls=%fused_computation.108 | custom fusion | bytes 12290 | tf_op jit(solution)/shard_map/scatter | solution.py:50
  89.9 7.3 all-to-all-start.1
  97.1 16.1 %scatter_custom_fusion.1 = s32[6144]{0:T(1024)} fusion(s32[4096]{0:T(1024)S(1)} %get-tuple-element.475, s32[4096]{0:T(1024)S(1)} %get-tuple-element.480, s32[]{:T(128)} %constant.283.clone.1), kind=kCustom, calls=%fused_computation.101 | custom fusion | bytes 24580 | tf_op jit(solution)/shard_map/scatter | solution.py:47
  113.2 6.0 all-to-all-start
  120.1 5.8 all-to-all-done
  126.0 262.1 %gather_fusion.1 = bf16[6144,4096]{1,0:T(8,128)(2,1)} fusion(bf16[4096,4096]{1,0:T(8,128)(2,1)} %bitcast.101, s32[6144]{0:T(1024)S(1)} %broadcast_clamp_fusion), kind=kCustom, calls=%fused_computation.1 | custom fusion | bytes 100687872 | tf_op jit(solution)/shard_map/jit(_take)/gather | solution.py:88
  388.1 33.4 %broadcast_select_fusion.2 = bf16[8,768,4096]{2,1,0:T(8,128)(2,1)} fusion(bf16[8,768,4096]{2,1,0:T(8,128)(2,1)} %bitcast.102, pred[8,768]{1,0:T(8,128)(4,1)S(1)} %compare_and_fusion), kind=kLoop, calls=%fused_computation.46 | loop fusion | flops 25165824 | bytes 100669440 | tf_op jit(solution)/shard_map/jit(_take)/select_n | solution.py:88
  421.5 44.3 %while.56 = (s32[]{:T(128)}, bf16[8,128,4096]{2,1,0:T(8,128)(2,1)}, s32[8,768]{1,0:T(8,128)S(1)}, bf16[8,768]{1,0:T(8,128)(2,1)}, bf16[8,768,4096]{2,1,0:T(8,128)(2,1)}, /*index=5*/s32[]{:T(128)}) while((s32[]{:T(128)}, bf16[8,128,4096]{2,1,0:T(8,128)(2,1)}, s32[8,768]{1,0:T(8,128)S(1)}, bf16[8,768]{1,0:T(8,128)(2,1)}, ...), condition=%wide.region_7.8_spmd, body=%wide.region_6.7_spmd.sunk | while | flops 805511424 | bytes 8403533 | solution.py:95
  465.9 159.1 %reduce-scatter.2.cloned.1.call-done = bf16[128,4096]{1,0:T(8,128)(2,1)} async-done(((bf16[1024,4096]{1,0:T(8,128)(2,1)}), bf16[128,4096]{1,0:T(8,128)(2,1)}) %reduce-scatter.2.cloned.1.call-update) | async-done | bytes 1048592 | tf_op jit(solution)/shard_map/reduce_scatter | solution.py:96
  625.1 5.2 all-gather.3
  630.3 29.8 %all-gather.7.cloned.1.call-done = bf16[512,4096]{1,0:T(8,128)(2,1)} async-done(((bf16[128,4096]{1,0:T(8,128)(2,1)}), bf16[512,4096]{1,0:T(8,128)(2,1)}) %all-gather.7.cloned.1.call-update) | async-done | bytes 4194320 | tf_op jit(solution)/shard_map/all_gather | solution.py:10
  660.1 10.5 %while.58 = (s32[]{:T(128)}, f32[1,4096]{1,0:T(1,128)S(1)}, f32[128,4096]{1,0:T(8,128)S(1)}, s32[]{:T(128)}, bf16[4,1,4096]{2,1,0:T(2,128)(2,1)S(1)}, /*index=5*/bf16[4,128,4096]{2,1,0:T(8,128)(2,1)}, s32[]{:T(128)}, s32[]{:T(128)}) while((s32[]{:T(128)}, f32[1,4096]{1,0:T(1,128)S(1)}, f32[128,4096]{1,0:T(8,128)S(1)}, ...), condition=%wide.region_10.11_spmd.clone, body=%wide.region_9.10_spmd.clone.sunk | while | flops 2637828 | bytes 5316723 | solution.py:28
  674.6 34.6 %all-gather.9.cloned.1.call-done = bf16[512,4096]{1,0:T(8,128)(2,1)} async-done(((bf16[128,4096]{1,0:T(8,128)(2,1)}), bf16[512,4096]{1,0:T(8,128)(2,1)}) %all-gather.9.cloned.1.call-update) | async-done | bytes 4194320 | tf_op jit(solution)/shard_map/all_gather | solution.py:10
  709.2 10.4 %while.59 = (s32[]{:T(128)}, f32[128,4096]{1,0:T(8,128)S(1)}, s32[]{:T(128)}, bf16[4,1,4096]{2,1,0:T(2,128)(2,1)S(1)}, bf16[4,128,4096]{2,1,0:T(8,128)(2,1)}, /*index=5*/s32[]{:T(128)}, s32[]{:T(128)}, s32[]{:T(128)}, s32[]{:T(128)}) while((s32[]{:T(128)}, f32[128,4096]{1,0:T(8,128)S(1)}, s32[]{:T(128)}, ...), condition=%wide.region_12.13_spmd.clone, body=%wide.region_11.12_spmd.clone.sunk | while | flops 2625544 | bytes 5284007 | solution.py:28
  729.9 42.1 %collective-permute-done = bf16[128,4096]{1,0:T(8,128)(2,1)} collective-permute-done((bf16[128,4096]{1,0:T(8,128)(2,1)S(1)}, bf16[128,4096]{1,0:T(8,128)(2,1)}, u32[]{:S(2)}, u32[]{:S(2)}) %collective-permute-start) | collective-permute-done | bytes 1048608 | tf_op jit(solution)/shard_map/ppermute | solution.py:121
  777.3 42.0 %collective-permute-done.2 = bf16[128,4096]{1,0:T(8,128)(2,1)S(1)} collective-permute-done((bf16[128,4096]{1,0:T(8,128)(2,1)}, bf16[128,4096]{1,0:T(8,128)(2,1)S(1)}, u32[]{:S(2)}, u32[]{:S(2)}) %collective-permute-start.2) | collective-permute-done | bytes 1048608 | tf_op jit(solution)/shard_map/ppermute | solution.py:121
  828.9 36.9 %collective-permute-done.4 = bf16[128,4096]{1,0:T(8,128)(2,1)S(1)} collective-permute-done((bf16[128,4096]{1,0:T(8,128)(2,1)S(1)}, bf16[128,4096]{1,0:T(8,128)(2,1)S(1)}, u32[]{:S(2)}, u32[]{:S(2)}) %collective-permute-start.4) | collective-permute-done | bytes 1048608 | tf_op jit(solution)/shard_map/ppermute | solution.py:121
  871.4 20.2 %collective-permute-done.6 = bf16[128,4096]{1,0:T(8,128)(2,1)S(1)} collective-permute-done((bf16[128,4096]{1,0:T(8,128)(2,1)S(1)}, bf16[128,4096]{1,0:T(8,128)(2,1)S(1)}, u32[]{:S(2)}, u32[]{:S(2)}) %collective-permute-start.6) | collective-permute-done | bytes 1048608 | tf_op jit(solution)/shard_map/ppermute | solution.py:121
  892.7 44.2 %while.57 = (s32[]{:T(128)}, f32[8,768]{1,0:T(8,128)S(1)}, s32[8,768]{1,0:T(8,128)S(1)}, bf16[8,128,4096]{2,1,0:T(8,128)(2,1)}, bf16[8,768,4096]{2,1,0:T(8,128)(2,1)}, /*index=5*/s32[]{:T(128)}, s32[]{:T(128)}) while((s32[]{:T(128)}, f32[8,768]{1,0:T(8,128)S(1)}, s32[8,768]{1,0:T(8,128)S(1)}, bf16[8,128,4096]{2,1,0:T(8,128)(2,1)}, ...), condition=%wide.region_15.16_spmd, body=%wide.region_13.15_spmd.sunk | while | flops 805608960 | bytes 7365717 | solution.py:134
  892.8 5.5 fusion.67
  898.4 5.3 fusion.67
  903.9 5.3 fusion.67
  909.4 5.3 fusion.67
  914.9 5.3 fusion.67
  920.4 5.3 fusion.67
  925.9 5.3 fusion.67
  931.4 5.3 fusion.67
  942.0 5.5 all-to-all-done.2
  947.4 23.0 %gather_fusion.2 = f32[4096]{0:T(1024)S(1)} fusion(f32[6144]{0:T(1024)S(1)} %bitcast.100, s32[4096]{0:T(1024)S(1)} %copy-done.8), kind=kCustom, calls=%fused_computation.2 | custom fusion | bytes 49152 | tf_op jit(solution)/shard_map/jit(_take)/gather | solution.py:136
  (148 shorter events, 118.4 us)
Async XLA Ops:
  14.9 44.3 %copy-start.9 = (bf16[1,128,32]{1,2,0:T(8,128)(2,1)S(1)}, bf16[1,128,32]{1,2,0:T(8,128)(2,1)}, u32[]{:S(2)}) copy-start(bf16[1,128,32]{1,2,0:T(8,128)(2,1)} %param.14) | copy-start | bytes 24580
  59.2 60.3 %copy-start.6 = (s32[4096]{0:T(1024)}, s32[4096]{0:T(1024)S(1)}, u32[]{:S(2)}) copy-start(s32[4096]{0:T(1024)S(1)} %get-tuple-element.475) | copy-start | bytes 49156
  89.9 23.4 %all-to-all-start.1 = ((bf16[8,2,384]{2,1,0:T(2,128)(2,1)}), bf16[8,2,384]{2,1,0:T(2,128)(2,1)S(1)}, u32[]{:S(2)}, u32[]{:S(2)}) async-start(bf16[8,2,384]{2,1,0:T(2,128)(2,1)} %reshape.367), calls=%async_computation.1 | async-start | bytes 24576 | tf_op jit(solution)/shard_map/all_to_all | solution.py:86
  113.2 12.6 %all-to-all-start = ((s32[8,1,768]{2,1,0:T(1,128)}), s32[8,1,768]{2,1,0:T(1,128)S(1)}, u32[]{:S(2)}, u32[]{:S(2)}) async-start(s32[8,1,768]{2,1,0:T(1,128)} %bitcast.18), calls=%async_computation | async-start | bytes 49152 | tf_op jit(solution)/shard_map/all_to_all | solution.py:85
  119.2 505.7 %reduce-scatter.2.cloned.1.call-start = ((), (), s32[]{:S(2)}) async-start(), calls=%async_computation.4 | async-start | bytes 9437184 | tf_op jit(solution)/shard_map/reduce_scatter | solution.py:96
  465.8 159.2 %copy-start.5 = (f32[1,4096]{1,0:T(1,128)S(1)}, f32[1,4096]{1,0:T(1,128)}, u32[]{:S(2)}) copy-start(f32[1,4096]{1,0:T(1,128)} %param.17) | copy-start | bytes 49156
  465.8 194.2 %all-gather.7.cloned.1.call-start = ((), (), s32[]{:S(2)}) async-start(), calls=%async_computation.5 | async-start | bytes 5242880 | tf_op jit(solution)/shard_map/all_gather | solution.py:10
  625.0 84.2 %all-gather.9.cloned.1.call-start = ((), (), s32[]{:S(2)}) async-start(), calls=%async_computation.6 | async-start | bytes 5242880 | tf_op jit(solution)/shard_map/all_gather | solution.py:10
  660.1 10.6 %copy-start.3 = (bf16[128,4096]{1,0:T(8,128)(2,1)S(1)}, bf16[128,4096]{1,0:T(8,128)(2,1)}, u32[]{:S(2)}) copy-start(bf16[128,4096]{1,0:T(8,128)(2,1)} %reduce-scatter.2.cloned.1.call-done) | copy-start | bytes 3145732
  719.6 1.6 copy-start.1
  719.6 1.8 copy-start.4
  722.0 3.2 copy-start
  725.2 46.8 %collective-permute-start = (bf16[128,4096]{1,0:T(8,128)(2,1)S(1)}, bf16[128,4096]{1,0:T(8,128)(2,1)}, u32[]{:S(2)}, u32[]{:S(2)}) collective-permute-start(bf16[128,4096]{1,0:T(8,128)(2,1)S(1)} %get-tuple-element.477), channel_id=1, source_target_pairs={{0,1},{1,2},{2,3},{3,4},{4,5},{5,6},{6,7},{7,0},{8,9},{9,10},{10,1... | collective-permute-start | bytes 3145736 | tf_op jit(solution)/shard_map/ppermute | solution.py:121
  726.6 47.9 %collective-permute-start.1 = (bf16[128,4096]{1,0:T(8,128)(2,1)S(1)}, bf16[128,4096]{1,0:T(8,128)(2,1)S(1)}, u32[]{:S(2)}, u32[]{:S(2)}) collective-permute-start(bf16[128,4096]{1,0:T(8,128)(2,1)S(1)} %get-tuple-element.477), channel_id=1, source_target_pairs={{0,7},{1,0},{2,1},{3,2},{4,3},{5,4},{6,5},{7,6},{8,15},{9,8},{10,9... | collective-permute-start | bytes 3145736 | tf_op jit(solution)/shard_map/ppermute | solution.py:126
  771.9 47.4 %collective-permute-start.2 = (bf16[128,4096]{1,0:T(8,128)(2,1)}, bf16[128,4096]{1,0:T(8,128)(2,1)S(1)}, u32[]{:S(2)}, u32[]{:S(2)}) collective-permute-start(bf16[128,4096]{1,0:T(8,128)(2,1)} %collective-permute-done), channel_id=1, source_target_pairs={{0,1},{1,2},{2,3},{3,4},{4,5},{5,6},{6,7},{7,0},{8,9},{9,10},{10,1... | collective-permute-start | bytes 3145736 | tf_op jit(solution)/shard_map/ppermute | solution.py:121
  774.5 50.5 %collective-permute-start.3 = (bf16[128,4096]{1,0:T(8,128)(2,1)S(1)}, bf16[128,4096]{1,0:T(8,128)(2,1)S(1)}, u32[]{:S(2)}, u32[]{:S(2)}) collective-permute-start(bf16[128,4096]{1,0:T(8,128)(2,1)S(1)} %collective-permute-done.1), channel_id=1, source_target_pairs={{0,7},{1,0},{2,1},{3,2},{4,3},{5,4},{6,5},{7,6},{8,15},{9,8},{10,9... | collective-permute-start | bytes 3145736 | tf_op jit(solution)/shard_map/ppermute | solution.py:126
  819.3 46.5 %collective-permute-start.4 = (bf16[128,4096]{1,0:T(8,128)(2,1)S(1)}, bf16[128,4096]{1,0:T(8,128)(2,1)S(1)}, u32[]{:S(2)}, u32[]{:S(2)}) collective-permute-start(bf16[128,4096]{1,0:T(8,128)(2,1)S(1)} %collective-permute-done.2), channel_id=1, source_target_pairs={{0,1},{1,2},{2,3},{3,4},{4,5},{5,6},{6,7},{7,0},{8,9},{9,10},{10,1... | collective-permute-start | bytes 3145736 | tf_op jit(solution)/shard_map/ppermute | solution.py:121
  825.1 45.3 %collective-permute-start.5 = (bf16[128,4096]{1,0:T(8,128)(2,1)S(1)}, bf16[128,4096]{1,0:T(8,128)(2,1)S(1)}, u32[]{:S(2)}, u32[]{:S(2)}) collective-permute-start(bf16[128,4096]{1,0:T(8,128)(2,1)S(1)} %collective-permute-done.3), channel_id=1, source_target_pairs={{0,7},{1,0},{2,1},{3,2},{4,3},{5,4},{6,5},{7,6},{8,15},{9,8},{10,9... | collective-permute-start | bytes 3145736 | tf_op jit(solution)/shard_map/ppermute | solution.py:126
  865.8 25.9 %collective-permute-start.6 = (bf16[128,4096]{1,0:T(8,128)(2,1)S(1)}, bf16[128,4096]{1,0:T(8,128)(2,1)S(1)}, u32[]{:S(2)}, u32[]{:S(2)}) collective-permute-start(bf16[128,4096]{1,0:T(8,128)(2,1)S(1)} %collective-permute-done.4), channel_id=1, source_target_pairs={{0,1},{1,2},{2,3},{3,4},{4,5},{5,6},{6,7},{7,0},{8,9},{9,10},{10,1... | collective-permute-start | bytes 3145736 | tf_op jit(solution)/shard_map/ppermute | solution.py:121
  892.7 48.1 %copy-start.2 = (f32[128,4096]{1,0:T(8,128)S(1)}, f32[128,4096]{1,0:T(8,128)}, u32[]{:S(2)}) copy-start(f32[128,4096]{1,0:T(8,128)} %get-tuple-element.479) | copy-start | bytes 6291460
  892.7 54.7 %copy-start.8 = (s32[4096]{0:T(1024)S(1)}, s32[4096]{0:T(1024)}, u32[]{:S(2)}) copy-start(s32[4096]{0:T(1024)} %get-tuple-element.474) | copy-start | bytes 49156
  937.5 9.9 %all-to-all-start.2 = ((f32[8,1,768]{2,1,0:T(1,128)}), f32[8,1,768]{2,1,0:T(1,128)S(1)}, u32[]{:S(2)}, u32[]{:S(2)}) async-start(f32[8,1,768]{2,1,0:T(1,128)} %all_to_all.31), calls=%async_computation.3 | async-start | bytes 49152 | tf_op jit(solution)/shard_map/all_to_all | solution.py:135
  947.4 23.0 %copy-start.7 = (s32[4096]{0:T(1024)S(1)}, s32[4096]{0:T(1024)}, u32[]{:S(2)}) copy-start(s32[4096]{0:T(1024)} %copy-done.6) | copy-start | bytes 49156
Sparse Core Ops, SparseCore 0:
  466.0 158.9 reduce-scatter.1
  626.6 33.4 all-gather.6
  674.7 34.4 all-gather.8
